TPU v7x, 32 devices: a whole 2x2x4 slice. The times are simulated.
32 devices in a mesh: dp: 8 (over y, x, core), tensor: 4 (over z).
Axes of the slice: x: 2, y: 2, z: 4, core: 2. Of those that a mesh axis runs over, the one named last changes fastest.
Arguments:
- teacher_master: float32 [256, 16384], P('dp', 'tensor'), as said below
- student_weight: bfloat16 [256, 16384], P('dp', 'tensor'), may hold values from -6 to 6
- teacher_feat: bfloat16 [2048, 256], P('dp'), as said below
- student_feat: bfloat16 [2048, 256], P('dp'), may hold values from -6 to 6
- center: float32 [16384], P('tensor'), may hold values from -0.3 to 0.3
Outputs:
- master_new: float32 [256, 16384], P('dp', 'tensor')
- student_grad: float32 [256, 16384], P('dp', 'tensor')
- new_center: float32 [16384], P('tensor')
Inputs may be any that keep to these rules, and one draw needn't show every extreme that they name: `teacher_feat`: rows of teacher features are real-valued and of order one. `teacher_master`: entries of the teacher master are real-valued and of order one.
All inputs are finite; a program needn't handle non-finite values.
Results may differ from a plain program's by a relative error of at most 0.014.
Values may be sent and summed in bfloat16 or wider, within the bound.
No kernel may reach another device: no remote copies, remote signals or barrier semaphores. Data moves between devices by JAX's collectives and lax.ppermute only.
A program may use at most 64 MiB of HBM per device.

v0:
```python
import jax
import jax.numpy as jnp
from jax import lax
from jax.sharding import PartitionSpec as P


def unit_rows(feat):
    wide = feat.astype(jnp.float32)
    return (wide * lax.rsqrt(jnp.sum(wide * wide, 1, keepdims=True) + 1e-06)).astype(jnp.bfloat16)


def shards(teacher_master, student_weight, teacher_feat, student_feat, center):
    zt = unit_rows(teacher_feat)
    zs = unit_rows(student_feat)
    images_all = teacher_feat.shape[0] * lax.axis_size("dp")
    student_full = lax.all_gather(student_weight, "dp", axis=0, tiled=True)
    master_new = 0.996 * teacher_master + 0.004 * student_weight.astype(jnp.float32)
    weight = lax.all_gather(master_new.astype(jnp.bfloat16), "dp", axis=0, tiled=True)
    feats = zt
    raw = jnp.dot(feats, weight, preferred_element_type=jnp.float32)
    squares = jnp.sum(jnp.square(weight.astype(jnp.float32)), 0)
    t_norm = jnp.sqrt(squares + 1e-06)
    t_cos = raw / t_norm
    s_norm = jnp.sqrt(jnp.sum(jnp.square(student_full.astype(jnp.float32)), 0) + 1e-06)
    s_cos = jnp.dot(zs, student_full, preferred_element_type=jnp.float32) / s_norm
    t_exp = jnp.exp((t_cos - center) / 0.04)
    s_exp = jnp.exp(s_cos / 0.1)
    t_total, s_total = lax.psum(
        (jnp.sum(t_exp, 1, keepdims=True), jnp.sum(s_exp, 1, keepdims=True)), "tensor"
    )
    cos_mean = lax.psum(jnp.sum(t_cos, 0), "dp") / images_all
    new_center = 0.5 * center + 0.5 * cos_mean
    dlog = ((s_exp / s_total - t_exp / t_total) / 0.1).astype(jnp.bfloat16)
    weighted = jnp.sum(dlog.astype(jnp.float32) * s_cos, 0)
    scaled = weighted / s_norm
    feats = zs
    product = lax.dot_general(
        feats, dlog, (((0,), (0,)), ((), ())), preferred_element_type=jnp.float32
    )
    student_grad = lax.psum_scatter(
        (product - student_full.astype(jnp.float32) * scaled) / s_norm,
        "dp",
        scatter_dimension=0,
        tiled=True,
    )
    return (master_new, student_grad, new_center)


def solution(mesh):
    placed = (P("dp", "tensor"), P("dp", "tensor"), P("dp", None), P("dp", None), P("tensor"))
    return jax.shard_map(
        shards,
        mesh=mesh,
        in_specs=placed,
        out_specs=(P("dp", "tensor"), P("dp", "tensor"), P("tensor")),
        check_vma=False,
    )
```

profile of v0, /device:TPU:0, one launch (start us, length us, event | category | flops | bytes accessed | tf_op | source)
XLA Modules:
  0.0 153.8 jit_solution(11268141412257356897)
XLA Ops:
  7.2 0.0 copy-start.3
  7.2 0.0 all-gather.3.cloned.1.call-start
  7.2 0.7 all-gather.3.cloned.1.call-update
  7.9 0.0 all-gather.5.cloned.1.call-start
  8.0 2.1 %fusion.13 = (bf16[32,4096]{1,0:T(8,128)(2,1)}, f32[32,4096]{1,0:T(8,128)}) fusion(bf16[32,4096]{1,0:T(8,128)(2,1)} %param.6, f32[32,4096]{1,0:T(8,128)} %param.5), kind=kLoop, calls=%fused_computation.31 | loop fusion | flops 655360 | bytes 1572864 | tf_op jit(solution)/shard_map/convert_element_type | solution.py:18
  10.0 0.0 all-gather.5.cloned.1.call-update
  10.1 0.0 reduce-scatter.2.cloned.1.call-start
  10.1 1.0 fusion.6
  11.1 1.0 fusion.4
  12.2 28.3 %all-gather.3.cloned.1.call-done = bf16[256,4096]{1,0:T(8,128)(2,1)} async-done(((bf16[32,4096]{1,0:T(8,128)(2,1)}), bf16[256,4096]{1,0:T(8,128)(2,1)}) %all-gather.3.cloned.1.call-update) | async-done | bytes 2097168 | tf_op jit(solution)/shard_map/all_gather | solution.py:16
  40.5 2.2 %fusion.1 = f32[4096]{0:T(1024)S(1)} fusion(bf16[256,4096]{1,0:T(8,128)(2,1)} %all-gather.3.cloned.1.call-done), kind=kLoop, calls=%fused_computation.6 | loop fusion | flops 3141632 | bytes 2113536 | tf_op jit(solution)/shard_map/reduce_sum | solution.py:24
  42.7 28.2 %all-gather.5.cloned.1.call-done = bf16[256,4096]{1,0:T(8,128)(2,1)} async-done(((bf16[32,4096]{1,0:T(8,128)(2,1)}), bf16[256,4096]{1,0:T(8,128)(2,1)}) %all-gather.5.cloned.1.call-update) | async-done | bytes 2097168 | tf_op jit(solution)/shard_map/all_gather | solution.py:18
  70.9 2.0 %multiply_reduce_fusion.1 = f32[4096]{0:T(1024)S(1)} fusion(bf16[256,4096]{1,0:T(8,128)(2,1)} %all-gather.5.cloned.1.call-done), kind=kLoop, calls=%fused_computation.10 | loop fusion | flops 3141632 | bytes 2113536 | tf_op jit(solution)/shard_map/reduce_sum | solution.py:21
  73.0 0.0 copy-start.2
  73.0 0.0 copy-start.4
  73.0 3.1 %fusion.2 = (f32[256]{0:T(256)S(1)}, f32[256,4096]{1,0:T(8,128)}) fusion(f32[4096]{0:T(1024)S(1)} %add_sqrt_fusion.1, bf16[256,4096]{1,0:T(8,128)(2,1)S(1)} %copy-done, bf16[256,256]{1,0:T(8,128)(2,1)S(1)} %copy-done.3, f32[256]{0:T(256)S(1)} %add_rsqrt_fusion.1), kind=kOutput, calls=%fused_computation.12 | convolution fusion | flops 540212992 | bytes 6440960 | tf_op jit(solution)/shard_map/dot_general | solution.py:25
  76.1 3.4 %fusion.12 = (f32[4096]{0:T(1024)S(1)}, f32[256]{0:T(256)S(1)}, f32[256,4096]{1,0:T(8,128)}) fusion(f32[4096]{0:T(1024)S(1)} %copy-done.4, f32[4096]{0:T(1024)S(1)} %add_sqrt_fusion, bf16[256,4096]{1,0:T(8,128)(2,1)S(1)} %copy-done.1, bf16[256,256]{1,0:T(8,128)(2,1)S(1)} %copy-done.2, f32[256]{0:T(256)S(1)} %add_rsqrt_fusion), kind=kOutput, calls=%fused_computation.30 | convolution fusion | flops 542306048 | bytes 6473728 | tf_op jit(solution)/shard_map/dot_general | solution.py:20
  79.5 11.7 %all-reduce = (f32[256]{0:T(256)S(1)}, f32[256]{0:T(256)S(1)}) all-reduce(f32[256]{0:T(256)S(1)} %get-tuple-element.4, f32[256]{0:T(256)S(1)} %get-tuple-element.12), channel_id=1, replica_groups=mesh['dp'=8,'tensor'=4] {'tensor'}, use_global_device_ids=true, to_apply=%region_7.0 | all-reduce | flops 512 | bytes 4096 | tf_op jit(solution)/shard_map/psum | solution.py:28
  91.1 4.5 %multiply_reduce_fusion = (f32[4096]{0:T(1024)S(1)}, bf16[256,4096]{1,0:T(8,128)(2,1)S(1)}) fusion(f32[256,4096]{1,0:T(8,128)} %get-tuple-element.13, f32[256]{0:T(256)S(1)} %get-tuple-element.5, f32[256,4096]{1,0:T(8,128)} %get-tuple-element.11, f32[4096]{0:T(1024)S(1)} %copy-done.4, f32[256]{0:T(256)S(1)} %get-tuple-element.6), kind=kLoop, calls=%fused_computation.7 | loop fusion | flops 11530240 | bytes 10520576 | tf_op jit(solution)/shard_map/reduce_sum | solution.py:34
  95.6 3.0 %fusion = f32[256,4096]{1,0:T(8,128)} fusion(bf16[256,4096]{1,0:T(8,128)(2,1)S(1)} %get-tuple-element.8, bf16[256,4096]{1,0:T(8,128)(2,1)S(1)} %copy-done, f32[4096]{0:T(1024)S(1)} %rsqrt_multiply_fusion, f32[4096]{0:T(1024)S(1)} %add_sqrt_fusion.1, bf16[256,256]{1,0:T(8,128)(2,1)S(1)} %copy-done.3, f32[256]{0:T(256)S(1)} %add_rsqrt_fusion.1), kind=kOutput, calls=%fused_computation.5 | convolution fusion | flops 541261824 | bytes 8553472 | tf_op jit(solution)/shard_map/dot_general | solution.py:37
  98.6 0.0 reduce-scatter.2.cloned.1.call-update
  98.6 22.4 %psum.23 = f32[4096]{0:T(1024)S(1)} all-reduce(f32[4096]{0:T(1024)S(1)} %get-tuple-element.3), channel_id=1, replica_groups=mesh['dp'=8,'tensor'=4] {'dp'}, use_global_device_ids=true, to_apply=%region_11.0 | all-reduce | flops 4096 | bytes 32768 | tf_op jit(solution)/shard_map/psum | solution.py:31
  121.0 0.6 multiply_add_fusion.1
  121.6 25.7 %reduce-scatter.2.cloned.1.call-done = f32[32,4096]{1,0:T(8,128)} async-done(((f32[256,4096]{1,0:T(8,128)}), f32[32,4096]{1,0:T(8,128)}) %reduce-scatter.2.cloned.1.call-update) | async-done | bytes 524304 | tf_op jit(solution)/shard_map/reduce_scatter | solution.py:40
  (12 shorter events, 0.1 us)
Async XLA Ops:
  7.2 65.8 %copy-start.3 = (bf16[256,256]{1,0:T(8,128)(2,1)S(1)}, bf16[256,256]{1,0:T(8,128)(2,1)}, u32[]{:S(2)}) copy-start(bf16[256,256]{1,0:T(8,128)(2,1)} %param.8) | copy-start | bytes 393220
  7.2 33.4 %all-gather.3.cloned.1.call-start = ((), (), s32[]{:S(2)}) async-start(), calls=%async_computation.1 | async-start | bytes 2359296 | tf_op jit(solution)/shard_map/all_gather | solution.py:16
  7.9 63.0 %all-gather.5.cloned.1.call-start = ((), (), s32[]{:S(2)}) async-start(), calls=%async_computation.2 | async-start | bytes 2359296 | tf_op jit(solution)/shard_map/all_gather | solution.py:18
  10.1 137.2 %reduce-scatter.2.cloned.1.call-start = ((), (), s32[]{:S(2)}) async-start(), calls=%async_computation.3 | async-start | bytes 4718592 | tf_op jit(solution)/shard_map/reduce_scatter | solution.py:40
  40.5 32.5 %copy-start = (bf16[256,4096]{1,0:T(8,128)(2,1)S(1)}, bf16[256,4096]{1,0:T(8,128)(2,1)}, u32[]{:S(2)}) copy-start(bf16[256,4096]{1,0:T(8,128)(2,1)} %all-gather.3.cloned.1.call-done) | copy-start | bytes 6291460
  73.0 3.1 %copy-start.1 = (bf16[256,4096]{1,0:T(8,128)(2,1)S(1)}, bf16[256,4096]{1,0:T(8,128)(2,1)}, u32[]{:S(2)}) copy-start(bf16[256,4096]{1,0:T(8,128)(2,1)} %all-gather.5.cloned.1.call-done) | copy-start | bytes 6291460
  73.0 3.1 %copy-start.2 = (bf16[256,256]{1,0:T(8,128)(2,1)S(1)}, bf16[256,256]{1,0:T(8,128)(2,1)}, u32[]{:S(2)}) copy-start(bf16[256,256]{1,0:T(8,128)(2,1)} %param.7) | copy-start | bytes 393220
  73.0 3.1 %copy-start.4 = (f32[4096]{0:T(1024)S(1)}, f32[4096]{0:T(1024)}, u32[]{:S(2)}) copy-start(f32[4096]{0:T(1024)} %param.9) | copy-start | bytes 49156
Sparse Core Ops, SparseCore 0:
  9.9 30.5 all-gather.2
  43.0 27.8 all-gather.4
  98.7 48.5 reduce-scatter.1
where the time goes:
time: 154 us
  waiting for transfers between devices  82.9 us (54%)
  blocking collectives  34.1 us (22%)
  between operations  13.9 us (9%)
  other arithmetic  13.4 us (9%)
  matrix products  9.39 us (6%)
    all_gather x1, waiting for transfers between devices, shards(): student_full = lax.all_gather(student_weight, 'dp', axis=0, tiled=True)  28.3 us
    all_gather x1, waiting for transfers between devices, shards(): lax.all_gather(master_new.astype(jnp.bfloat16), 'dp', axis=0, tiled=True)  28.2 us
    reduce_scatter x1, waiting for transfers between devices, shards(): lax.psum_scatter((product - student_full.astype(jnp.float32) * scaled) /...  25.7 us
    psum x1, blocking collectives, shards(): cos_mean = lax.psum(jnp.sum(t_cos, 0), 'dp') / images_all  22.4 us
    psum x1, blocking collectives, shards(): lax.psum((jnp.sum(t_exp, 1, keepdims=True), jnp.sum(s_exp, 1, keepdims=Tr...  11.7 us
    reduce_sum x1, other arithmetic, shards(): weighted = jnp.sum(dlog.astype(jnp.float32) * s_cos, 0)  4.47 us
    dot_general x1, matrix products, shards(): raw = jnp.dot(feats, weight, preferred_element_type=jnp.float32)  3.37 us
  transfers between devices with their start and end apart: 3, of which 3 were waited for; matrix products, arithmetic and copies ran while one was open for 5% of the time, Pallas kernels for 0%

commit v1 on v0

--- a/solution.py
+++ b/solution.py
@@ -13,7 +13,14 @@
     zt = unit_rows(teacher_feat)
     zs = unit_rows(student_feat)
     images_all = teacher_feat.shape[0] * lax.axis_size("dp")
-    student_full = lax.all_gather(student_weight, "dp", axis=0, tiled=True)
+    ways, here, step = (lax.axis_size("dp"), lax.axis_index("dp"), student_weight.shape[0])
+    line, have = (student_weight, 1)
+    while have < ways:
+        line = jnp.concatenate(
+            [line, lax.ppermute(line, "dp", [(d, (d - have) % ways) for d in range(ways)])], axis=0
+        )
+        have = 2 * have
+    student_full = jnp.roll(line, here * step, axis=0)
     master_new = 0.996 * teacher_master + 0.004 * student_weight.astype(jnp.float32)
     weight = lax.all_gather(master_new.astype(jnp.bfloat16), "dp", axis=0, tiled=True)
     feats = zt

time: 154 us -> 152 us (0.987)
  waiting for transfers between devices: 82.9 us -> 70.6 us
  starting transfers between devices: 0.12 us -> 4.86 us
  local copies, waits for them, and re-layouts: 0.03 us -> 2.73 us
  matrix products: 9.39 us -> 11.1 us
    ppermute x0 -> x3, waiting for transfers between devices: none -> 45 us  [shards(): lax.ppermute(line, 'dp', [(d, (d - have) % ways) for d in range(ways)])]
    all_gather x1 -> x0, waiting for transfers between devices: 28.3 us -> none  [shards(): student_full = lax.all_gather(student_weight, 'dp', axis=0, tiled=True)]
    all_gather x1, waiting for transfers between devices: 28.2 us -> 0.01 us  [shards(): lax.all_gather(master_new.astype(jnp.bfloat16), 'dp', axis=0, tiled=True)]
    ppermute x0 -> x3, starting transfers between devices: none -> 4.79 us  [shards(): lax.ppermute(line, 'dp', [(d, (d - have) % ways) for d in range(ways)])]
    unnamed x10 -> x19, local copies, waits for them, and re-layouts: 0.03 us -> 2.65 us
    concatenate x0 -> x2, other arithmetic: none -> 2.02 us  [shards(): jnp.concatenate([line, lax.ppermute(line, 'dp', [(d, (d - have) % ways) f...]
    reduce_sum x1, other arithmetic: 2.18 us -> 0.45 us  [shards(): jnp.sum(jnp.square(student_full.astype(jnp.float32)), 0) + 1e-06]
    dot_general x1, matrix products: 3.37 us -> 4.94 us  [shards(): raw = jnp.dot(feats, weight, preferred_element_type=jnp.float32)]
  transfers between devices with their start and end apart: 3 -> 5, of which waited for: 3 -> 4; matrix products, arithmetic and copies ran while one was open for 5% -> 8% of each run, Pallas kernels for 0% -> 0%
where the time goes in v1:
time: 152 us
  waiting for transfers between devices  70.6 us (46%)
  blocking collectives  34.3 us (23%)
  between operations  14.2 us (9%)
  other arithmetic  13.9 us (9%)
  matrix products  11.1 us (7%)
  starting transfers between devices  4.86 us (3%)
  local copies, waits for them, and re-layouts  2.73 us (2%)
    ppermute x3, waiting for transfers between devices, shards(): lax.ppermute(line, 'dp', [(d, (d - have) % ways) for d in range(ways)])  45 us
    reduce_scatter x1, waiting for transfers between devices, shards(): lax.psum_scatter((product - student_full.astype(jnp.float32) * scaled) /...  25.6 us
    psum x1, blocking collectives, shards(): cos_mean = lax.psum(jnp.sum(t_cos, 0), 'dp') / images_all  22.4 us
    psum x1, blocking collectives, shards(): lax.psum((jnp.sum(t_exp, 1, keepdims=True), jnp.sum(s_exp, 1, keepdims=Tr...  11.9 us
    dot_general x1, matrix products, shards(): raw = jnp.dot(feats, weight, preferred_element_type=jnp.float32)  4.94 us
    ppermute x3, starting transfers between devices, shards(): lax.ppermute(line, 'dp', [(d, (d - have) % ways) for d in range(ways)])  4.79 us
    reduce_sum x1, other arithmetic, shards(): weighted = jnp.sum(dlog.astype(jnp.float32) * s_cos, 0)  4.61 us
    dot_general x1, matrix products, shards(): jnp.dot(zs, student_full, preferred_element_type=jnp.float32) / s_norm  3.13 us
  transfers between devices with their start and end apart: 5, of which 4 were waited for; matrix products, arithmetic and copies ran while one was open for 8% of the time, Pallas kernels for 0%

profile of v1, /device:TPU:0, one launch (start us, length us, event | category | flops | bytes accessed | tf_op | source)
XLA Modules:
  0.0 151.7 jit_solution(2176392929709355145)
XLA Ops:
  7.2 3.4 %collective-permute-start = (bf16[32,4096]{1,0:T(8,128)(2,1)}, bf16[32,4096]{1,0:T(8,128)(2,1)S(1)}, u32[]{:S(2)}, u32[]{:S(2)}) collective-permute-start(bf16[32,4096]{1,0:T(8,128)(2,1)} %param.6), channel_id=1, source_target_pairs={{0,28},{4,0},{8,4},{12,8},{16,12},{20,16},{24,20},{28,24},{1,29},{... | collective-permute-start | bytes 786440 | tf_op jit(solution)/shard_map/ppermute | solution.py:20
  10.6 2.1 %fusion.19 = (bf16[32,4096]{1,0:T(8,128)(2,1)}, f32[32,4096]{1,0:T(8,128)}) fusion(bf16[32,4096]{1,0:T(8,128)(2,1)} %param.6, f32[32,4096]{1,0:T(8,128)} %param.5), kind=kLoop, calls=%fused_computation.44 | loop fusion | flops 655360 | bytes 1572864 | tf_op jit(solution)/shard_map/convert_element_type | solution.py:25
  12.7 1.0 fusion.8
  13.8 1.0 collective-permute-done
  14.8 1.0 pad_maximum_fusion.1
  15.8 0.6 collective-permute-start.1
  16.4 1.0 fusion.6
  17.4 1.0 constant_dynamic-update-slice_fusion.7
  18.4 14.5 %collective-permute-done.1 = bf16[64,4096]{1,0:T(8,128)(2,1)S(1)} collective-permute-done((bf16[64,4096]{1,0:T(8,128)(2,1)S(1)}, bf16[64,4096]{1,0:T(8,128)(2,1)S(1)}, u32[]{:S(2)}, u32[]{:S(2)}) %collective-permute-start.1) | collective-permute-done | bytes 524320 | tf_op jit(solution)/shard_map/ppermute | solution.py:20
  32.9 1.0 pad_maximum_fusion
  33.9 0.8 collective-permute-start.2
  34.8 29.5 %collective-permute-done.2 = bf16[128,4096]{1,0:T(8,128)(2,1)S(1)} collective-permute-done((bf16[128,4096]{1,0:T(8,128)(2,1)S(1)}, bf16[128,4096]{1,0:T(8,128)(2,1)S(1)}, u32[]{:S(2)}, u32[]{:S(2)}) %collective-permute-start.2) | collective-permute-done | bytes 1048608 | tf_op jit(solution)/shard_map/ppermute | solution.py:20
  64.5 0.1 constant_dynamic-update-slice_fusion
  64.6 0.4 fusion
  65.0 1.4 copy-done.1
  66.5 3.1 %fusion.3 = (f32[256]{0:T(256)S(1)}, f32[256,4096]{1,0:T(8,128)}) fusion(f32[4096]{0:T(1024)S(1)} %add_sqrt_fusion.1, bf16[512,4096]{1,0:T(8,128)(2,1)S(1)} %constant_dynamic-update-slice_fusion, s32[]{:T(128)S(6)} %select_n.14, bf16[256,256]{1,0:T(8,128)(2,1)S(1)} %copy-done.4, f32[256]{0:T(256)S(1)} %add_rsqrt_fusion.1), kind=kOutput, calls=%fused_computation.12 | convolution fusion | flops 540212992 | bytes 6440964 | tf_op jit(solution)/shard_map/dot_general | solution.py:32
  69.6 2.0 %multiply_reduce_fusion.1 = f32[4096]{0:T(1024)S(1)} fusion(bf16[256,4096]{1,0:T(8,128)(2,1)} %all-gather.2.cloned.1.call-done), kind=kLoop, calls=%fused_computation.10 | loop fusion | flops 3141632 | bytes 2113536 | tf_op jit(solution)/shard_map/reduce_sum | solution.py:28
  71.7 4.9 %fusion.18 = (f32[4096]{0:T(1024)S(1)}, f32[256]{0:T(256)S(1)}, f32[256,4096]{1,0:T(8,128)}) fusion(f32[4096]{0:T(1024)S(1)} %copy-done.5, f32[4096]{0:T(1024)S(1)} %add_sqrt_fusion, bf16[256,4096]{1,0:T(8,128)(2,1)} %all-gather.2.cloned.1.call-done, bf16[256,256]{1,0:T(8,128)(2,1)S(1)} %copy-done.3, f32[256]{0:T(256)S(1)} %add_rsqrt_fusion), kind=kOutput, calls=%fused_computation.43 | convolution fusion | flops 542306048 | bytes 6473728 | tf_op jit(solution)/shard_map/dot_general | solution.py:27
  76.6 11.9 %all-reduce = (f32[256]{0:T(256)S(1)}, f32[256]{0:T(256)S(1)}) all-reduce(f32[256]{0:T(256)S(1)} %get-tuple-element.4, f32[256]{0:T(256)S(1)} %get-tuple-element.12), channel_id=1, replica_groups=mesh['dp'=8,'tensor'=4] {'tensor'}, use_global_device_ids=true, to_apply=%region_7.8 | all-reduce | flops 512 | bytes 4096 | tf_op jit(solution)/shard_map/psum | solution.py:35
  88.6 4.6 %multiply_reduce_fusion = (f32[4096]{0:T(1024)S(1)}, bf16[256,4096]{1,0:T(8,128)(2,1)S(1)}) fusion(f32[256,4096]{1,0:T(8,128)} %get-tuple-element.13, f32[256]{0:T(256)S(1)} %get-tuple-element.5, f32[256,4096]{1,0:T(8,128)} %get-tuple-element.11, f32[4096]{0:T(1024)S(1)} %copy-done.5, f32[256]{0:T(256)S(1)} %get-tuple-element.6), kind=kLoop, calls=%fused_computation.7 | loop fusion | flops 11530240 | bytes 10520576 | tf_op jit(solution)/shard_map/reduce_sum | solution.py:41
  93.2 3.0 %fusion.2 = f32[256,4096]{1,0:T(8,128)} fusion(f32[4096]{0:T(1024)S(1)} %rsqrt_multiply_fusion, f32[4096]{0:T(1024)S(1)} %add_sqrt_fusion.1, bf16[512,4096]{1,0:T(8,128)(2,1)S(1)} %copy-done.2, s32[]{:T(128)S(6)} %select_n.14, bf16[256,4096]{1,0:T(8,128)(2,1)S(1)} %get-tuple-element.8, bf16[256,256]{1,0:T(8,128)(2,1)S(1)} %copy-done.4, ...), kind=kOutput, calls=%fused_computation.6 | convolution fusion | flops 541261824 | bytes 8553476 | tf_op jit(solution)/shard_map/dot_general | solution.py:44
  96.2 22.4 %psum.23 = f32[4096]{0:T(1024)S(1)} all-reduce(f32[4096]{0:T(1024)S(1)} %get-tuple-element.3), channel_id=1, replica_groups=mesh['dp'=8,'tensor'=4] {'dp'}, use_global_device_ids=true, to_apply=%region_11.12 | all-reduce | flops 4096 | bytes 32768 | tf_op jit(solution)/shard_map/psum | solution.py:38
  118.6 0.6 multiply_add_fusion.1
  119.3 25.6 %reduce-scatter.2.cloned.1.call-done = f32[32,4096]{1,0:T(8,128)} async-done(((f32[256,4096]{1,0:T(8,128)}), f32[32,4096]{1,0:T(8,128)}) %reduce-scatter.2.cloned.1.call-update) | async-done | bytes 524304 | tf_op jit(solution)/shard_map/reduce_scatter | solution.py:47
  (27 shorter events, 0.4 us)
Async XLA Ops:
  7.2 62.5 %all-gather.2.cloned.1.call-start = ((), (), s32[]{:S(2)}) async-start(), calls=%async_computation.1 | async-start | bytes 2359296 | tf_op jit(solution)/shard_map/all_gather | solution.py:25
  7.2 7.6 %collective-permute-start = (bf16[32,4096]{1,0:T(8,128)(2,1)}, bf16[32,4096]{1,0:T(8,128)(2,1)S(1)}, u32[]{:S(2)}, u32[]{:S(2)}) collective-permute-start(bf16[32,4096]{1,0:T(8,128)(2,1)} %param.6), channel_id=1, source_target_pairs={{0,28},{4,0},{8,4},{12,8},{16,12},{20,16},{24,20},{28,24},{1,29},{... | collective-permute-start | bytes 786440 | tf_op jit(solution)/shard_map/ppermute | solution.py:20
  12.7 51.7 %copy-start = (bf16[32,4096]{1,0:T(8,128)(2,1)S(1)}, bf16[32,4096]{1,0:T(8,128)(2,1)}, u32[]{:S(2)}) copy-start(bf16[32,4096]{1,0:T(8,128)(2,1)} %param.6) | copy-start | bytes 786436
  12.7 132.2 %reduce-scatter.2.cloned.1.call-start = ((), (), s32[]{:S(2)}) async-start(), calls=%async_computation.2 | async-start | bytes 4718592 | tf_op jit(solution)/shard_map/reduce_scatter | solution.py:47
  15.8 17.1 %collective-permute-start.1 = (bf16[64,4096]{1,0:T(8,128)(2,1)S(1)}, bf16[64,4096]{1,0:T(8,128)(2,1)S(1)}, u32[]{:S(2)}, u32[]{:S(2)}) collective-permute-start(bf16[64,4096]{1,0:T(8,128)(2,1)S(1)} %pad_maximum_fusion.1), channel_id=1, source_target_pairs={{0,24},{4,28},{8,0},{12,4},{16,8},{20,12},{24,16},{28,20},{1,25},{... | collective-permute-start | bytes 1572872 | tf_op jit(solution)/shard_map/ppermute | solution.py:20
  33.9 30.4 %collective-permute-start.2 = (bf16[128,4096]{1,0:T(8,128)(2,1)S(1)}, bf16[128,4096]{1,0:T(8,128)(2,1)S(1)}, u32[]{:S(2)}, u32[]{:S(2)}) collective-permute-start(bf16[128,4096]{1,0:T(8,128)(2,1)S(1)} %pad_maximum_fusion), channel_id=1, source_target_pairs={{0,16},{4,20},{8,24},{12,28},{16,0},{20,4},{24,8},{28,12},{1,17},{... | collective-permute-start | bytes 3145736 | tf_op jit(solution)/shard_map/ppermute | solution.py:20
  34.8 31.7 %copy-start.4 = (bf16[256,256]{1,0:T(8,128)(2,1)S(1)}, bf16[256,256]{1,0:T(8,128)(2,1)}, u32[]{:S(2)}) copy-start(bf16[256,256]{1,0:T(8,128)(2,1)} %param.8) | copy-start | bytes 393220
  64.6 1.9 %copy-start.1 = (bf16[512,4096]{1,0:T(8,128)(2,1)}, bf16[512,4096]{1,0:T(8,128)(2,1)S(1)}, u32[]{:S(2)}) copy-start(bf16[512,4096]{1,0:T(8,128)(2,1)S(1)} %constant_dynamic-update-slice_fusion) | copy-start | bytes 12582916
  66.5 5.2 %copy-start.3 = (bf16[256,256]{1,0:T(8,128)(2,1)S(1)}, bf16[256,256]{1,0:T(8,128)(2,1)}, u32[]{:S(2)}) copy-start(bf16[256,256]{1,0:T(8,128)(2,1)} %param.7) | copy-start | bytes 393220
  66.5 5.2 %copy-start.5 = (f32[4096]{0:T(1024)S(1)}, f32[4096]{0:T(1024)}, u32[]{:S(2)}) copy-start(f32[4096]{0:T(1024)} %param.9) | copy-start | bytes 49156
  88.6 4.7 %copy-start.2 = (bf16[512,4096]{1,0:T(8,128)(2,1)S(1)}, bf16[512,4096]{1,0:T(8,128)(2,1)}, u32[]{:S(2)}) copy-start(bf16[512,4096]{1,0:T(8,128)(2,1)} %copy-done.1) | copy-start | bytes 12582916
Sparse Core Ops, SparseCore 0:
  12.8 38.3 all-gather.1
  96.4 48.4 reduce-scatter.1
